TPU v7x, 128 devices: a whole 4x4x4 slice. The times are simulated.
128 devices in a mesh: tm: 16 (over z_hi, y, core), tensor: 8 (over z_lo, x).
Axes of the slice: x: 4, y: 4, z: 4 (z_hi: 2, z_lo: 2; z = z_hi * 2 + z_lo), core: 2. Of those that a mesh axis runs over, the one named last changes fastest.
Arguments:
- hidden_in: bfloat16 [16, 2, 256, 5120], P('tm', None, None, 'tensor'), may hold values from -6 to 6
- noisy_queries: bfloat16 [16, 2, 256, 5120], P('tm', None, None, 'tensor'), may hold values from -28 to 28
- noisy_keys: bfloat16 [16, 2, 256, 5120], P('tm', None, None, 'tensor'), may hold values from -5 to 5
- noisy_values: bfloat16 [16, 2, 256, 5120], P('tm', None, None, 'tensor'), may hold values from -15 to 15
- clean_cache: bfloat16 [16, 2, 256, 5120], P('tm', None, None, 'tensor'), may hold values from -9 to 9
- out_proj: bfloat16 [5120, 5120], P('tensor'), may hold values from -0.078125 to 0.078125
- branch_in: bfloat16 [5120, 2560], P(None, 'tensor'), may hold values from -0.078125 to 0.078125
- branch_out: bfloat16 [2560, 5120], P('tensor'), may hold values from -0.125 to 0.125
- action_table: bfloat16 [128, 2560], P(None, 'tensor'), may hold values from -6 to 6
- actions: int32 [16, 4], P('tm'), may hold values from 0 to 127
- offsets: int32 [16], P('tm'), may hold values from 0 to 2, as said below
- out_grad: bfloat16 [16, 2, 256, 5120], P('tm', None, None, 'tensor'), may hold values from -6 to 6
Outputs:
- layer_out: bfloat16 [16, 2, 256, 5120], P('tm', None, None, 'tensor')
- input_grad: bfloat16 [16, 2, 256, 5120], P('tm', None, None, 'tensor')
- query_grad: bfloat16 [16, 2, 256, 5120], P('tm', None, None, 'tensor')
- key_grad: bfloat16 [16, 2, 256, 5120], P('tm', None, None, 'tensor')
- value_grad: bfloat16 [16, 2, 256, 5120], P('tm', None, None, 'tensor')
- cache_grad: float32 [16, 2, 256, 5120], P('tm', None, None, 'tensor')
- proj_weight_grad: float32 [5120, 5120], P('tensor', 'tm')
- branch_in_grad: float32 [5120, 2560], P('tm', 'tensor')
- branch_out_grad: float32 [2560, 5120], P('tensor', 'tm')
- table_grad: float32 [128, 2560], P('tm', 'tensor')
Inputs may be any that keep to these rules, and one draw needn't show every extreme that they name: offsets[c] <= c; spans 1, 2, 7, 8, 9 and the last reach min(c, 2).
All inputs are finite; a program needn't handle non-finite values.
Results may differ from a plain program's by a relative error of at most 0.013.
Values may be sent and summed in bfloat16 or wider, within the bound.
No kernel may reach another device: no remote copies, remote signals or barrier semaphores. Data moves between devices by JAX's collectives and lax.ppermute only.
A program may use at most 192 MiB of HBM per device.

v0:
```python
import jax
import jax.numpy as jnp
from jax import lax
from jax.sharding import PartitionSpec as P

HD = 128
GELU_C = 0.7978845608028654
GELU_A = 0.044715


def from_behind(value, axis, steps):
    count = lax.axis_size(axis)
    first, last = (max(0, -steps), min(count, count - steps))
    return lax.ppermute(value, axis, [(source, source + steps) for source in range(first, last)])


def gelu_value(inputs):
    inner = GELU_C * (inputs + GELU_A * inputs * inputs * inputs)
    return 0.5 * inputs * (1.0 + jnp.tanh(inner))


def gelu_slope(inputs):
    tangent = jnp.tanh(GELU_C * (inputs + GELU_A * inputs * inputs * inputs))
    return 0.5 * (1.0 + tangent) + 0.5 * inputs * (1.0 - tangent * tangent) * GELU_C * (
        1.0 + 3.0 * GELU_A * inputs * inputs
    )


def contract_rows(left, right):
    return lax.dot_general(
        left, right, (((0,), (0,)), ((), ())), preferred_element_type=jnp.float32
    )


def contract_cols(left, right):
    return lax.dot_general(
        left, right, (((1,), (1,)), ((), ())), preferred_element_type=jnp.float32
    )


def body(
    hidden_in,
    noisy_queries,
    noisy_keys,
    noisy_values,
    clean_cache,
    out_proj,
    branch_in,
    branch_out,
    action_table,
    actions,
    offsets,
    out_grad,
):
    steps_here = noisy_queries.shape[1]
    tokens_here = noisy_queries.shape[2]
    head_width = noisy_queries.shape[3]
    heads_here = head_width // HD
    model_width = out_proj.shape[1]
    row_count = steps_here * tokens_here
    action_count = actions.shape[1]
    score_scale = HD ** (-0.5)
    full_both = lax.all_gather(
        jnp.concatenate([hidden_in, out_grad], axis=0), "tensor", axis=3, tiled=True
    )
    input_rows = full_both[0].reshape(row_count, model_width)
    grad_rows = full_both[1].reshape(row_count, model_width)
    own_cache = clean_cache[0]
    nearer = from_behind(own_cache, "tm", 1)
    farther = from_behind(own_cache, "tm", 2)
    reach = offsets[0]
    allowed = jnp.concatenate(
        [
            jnp.full((tokens_here,), reach >= 2),
            jnp.full((tokens_here,), reach >= 1),
            jnp.ones((tokens_here,), bool),
        ]
    )
    block_shape = (steps_here, tokens_here, head_width)
    key_block = jnp.concatenate(
        [
            jnp.broadcast_to(farther[0], block_shape),
            jnp.broadcast_to(nearer[0], block_shape),
            noisy_keys[0],
        ],
        axis=1,
    )
    value_block = jnp.concatenate(
        [
            jnp.broadcast_to(farther[1], block_shape),
            jnp.broadcast_to(nearer[1], block_shape),
            noisy_values[0],
        ],
        axis=1,
    )
    query_heads = noisy_queries[0].reshape(steps_here, tokens_here, heads_here, HD)
    key_heads = key_block.reshape(steps_here, 3 * tokens_here, heads_here, HD)
    value_heads = value_block.reshape(steps_here, 3 * tokens_here, heads_here, HD)
    scores = (
        jnp.einsum("sqhe,skhe->shqk", query_heads, key_heads, preferred_element_type=jnp.float32)
        * score_scale
    )
    masked = jnp.where(allowed[None, None, None, :], scores, -1e30)
    largest = jnp.max(masked, axis=-1, keepdims=True)
    raised = jnp.exp(masked - largest)
    probs = raised / jnp.sum(raised, axis=-1, keepdims=True)
    probs_low = probs.astype(jnp.bfloat16)
    attended = (
        jnp.einsum("shqk,skhe->sqhe", probs_low, value_heads, preferred_element_type=jnp.float32)
        .astype(jnp.bfloat16)
        .reshape(row_count, head_width)
    )
    onehot = (actions[0][:, None] == jnp.arange(action_table.shape[0])[None, :]).astype(
        jnp.bfloat16
    )
    action_rows = jnp.dot(onehot, action_table, preferred_element_type=jnp.float32)
    branch_width = branch_in.shape[1]
    pre_act = (
        jnp.dot(input_rows, branch_in, preferred_element_type=jnp.float32).reshape(
            steps_here, action_count, tokens_here // action_count, branch_width
        )
        + action_rows[None, :, None, :]
    )
    pre_act = pre_act.reshape(row_count, branch_width)
    branch_act = gelu_value(pre_act).astype(jnp.bfloat16)
    partial_value = jnp.dot(attended, out_proj, preferred_element_type=jnp.float32) + jnp.dot(
        branch_act, branch_out, preferred_element_type=jnp.float32
    )
    layer_sum = lax.psum_scatter(
        partial_value.reshape(1, steps_here, tokens_here, model_width).astype(jnp.bfloat16),
        "tensor",
        scatter_dimension=3,
        tiled=True,
    ).astype(jnp.float32)
    layer_out = (hidden_in.astype(jnp.float32) + layer_sum).astype(jnp.bfloat16)
    attended_grad = contract_cols(grad_rows, out_proj).astype(jnp.bfloat16)
    pre_grad = (contract_cols(grad_rows, branch_out) * gelu_slope(pre_act)).astype(jnp.bfloat16)
    tm_count = lax.axis_size("tm")
    col_block = model_width // tm_count
    grad_split = grad_rows.reshape(row_count, tm_count, col_block)
    in_term = jnp.einsum(
        "rjk,rn->jkn",
        input_rows.reshape(row_count, tm_count, model_width // tm_count),
        pre_grad,
        preferred_element_type=jnp.float32,
    )
    out_term = jnp.einsum("rk,rjn->jkn", branch_act, grad_split, preferred_element_type=jnp.float32)
    grouped = jnp.sum(
        pre_grad.reshape(
            steps_here, action_count, tokens_here // action_count, branch_width
        ).astype(jnp.float32),
        axis=(0, 2),
    )
    table_term = jnp.dot(onehot.astype(jnp.float32).T, grouped, precision=lax.Precision.HIGHEST)
    proj_term = jnp.einsum("rk,rjn->jkn", attended, grad_split, preferred_element_type=jnp.float32)
    table_rows = table_term.shape[0] // tm_count
    pieces = (
        proj_term.astype(jnp.bfloat16),
        in_term.astype(jnp.bfloat16),
        out_term.astype(jnp.bfloat16),
        table_term.reshape(tm_count, table_rows, branch_width).astype(jnp.bfloat16),
    )
    merged = lax.psum_scatter(
        jnp.concatenate(pieces, axis=1), "tm", scatter_dimension=0, tiled=True
    )[0].astype(jnp.float32)
    bounds = [0]
    for piece in pieces:
        bounds.append(bounds[-1] + piece.shape[1])
    summed = tuple((merged[bounds[i] : bounds[i + 1]] for i in range(4)))
    input_term = contract_cols(pre_grad, branch_in)
    input_sum = lax.psum_scatter(
        input_term.reshape(1, steps_here, tokens_here, model_width).astype(jnp.bfloat16),
        "tensor",
        scatter_dimension=3,
        tiled=True,
    ).astype(jnp.float32)
    input_grad = (out_grad.astype(jnp.float32) + input_sum).astype(jnp.bfloat16)
    weight_grads = (summed, input_grad)
    grad_heads = attended_grad.reshape(steps_here, tokens_here, heads_here, HD)
    value_all = jnp.einsum(
        "shqk,sqhe->skhe", probs_low, grad_heads, preferred_element_type=jnp.float32
    )
    prob_grad = jnp.einsum(
        "sqhe,skhe->shqk", grad_heads, value_heads, preferred_element_type=jnp.float32
    )
    centre = jnp.sum(prob_grad * probs, axis=-1, keepdims=True)
    score_grad = (probs * (prob_grad - centre) * score_scale).astype(jnp.bfloat16)
    query_grad = (
        jnp.einsum("shqk,skhe->sqhe", score_grad, key_heads, preferred_element_type=jnp.float32)
        .astype(jnp.bfloat16)
        .reshape(1, steps_here, tokens_here, head_width)
    )
    key_all = jnp.einsum(
        "shqk,sqhe->skhe", score_grad, query_heads, preferred_element_type=jnp.float32
    ).reshape(steps_here, 3 * tokens_here, head_width)
    value_all = value_all.reshape(steps_here, 3 * tokens_here, head_width)
    own_key = key_all[:, 2 * tokens_here :].astype(jnp.bfloat16)[None]
    own_value = value_all[:, 2 * tokens_here :].astype(jnp.bfloat16)[None]
    toward_far = jnp.stack(
        [jnp.sum(key_all[:, :tokens_here], axis=0), jnp.sum(value_all[:, :tokens_here], axis=0)]
    )
    toward_near = jnp.stack(
        [
            jnp.sum(key_all[:, tokens_here : 2 * tokens_here], axis=0),
            jnp.sum(value_all[:, tokens_here : 2 * tokens_here], axis=0),
        ]
    )
    from_next = from_behind(toward_near.astype(jnp.bfloat16), "tm", -1).astype(toward_near.dtype)
    from_after = from_behind(toward_far.astype(jnp.bfloat16), "tm", -2).astype(toward_far.dtype)
    received = from_next + from_after
    attention_grads = (query_grad, own_key, own_value, received[None])
    summed, input_grad = weight_grads
    query_grad, own_key, own_value, cache_grad = attention_grads
    return (
        layer_out,
        input_grad,
        query_grad,
        own_key,
        own_value,
        cache_grad,
        summed[0],
        summed[1],
        summed[2],
        summed[3],
    )


def solution(mesh):
    in_specs = (
        P("tm", None, None, "tensor"),
        P("tm", None, None, "tensor"),
        P("tm", None, None, "tensor"),
        P("tm", None, None, "tensor"),
        P("tm", None, None, "tensor"),
        P("tensor", None),
        P(None, "tensor"),
        P("tensor", None),
        P(None, "tensor"),
        P("tm", None),
        P("tm"),
        P("tm", None, None, "tensor"),
    )
    out_specs = (
        P("tm", None, None, "tensor"),
        P("tm", None, None, "tensor"),
        P("tm", None, None, "tensor"),
        P("tm", None, None, "tensor"),
        P("tm", None, None, "tensor"),
        P("tm", None, None, "tensor"),
        P("tensor", "tm"),
        P("tm", "tensor"),
        P("tensor", "tm"),
        P("tm", "tensor"),
    )
    return jax.shard_map(body, mesh=mesh, in_specs=in_specs, out_specs=out_specs, check_vma=False)
```

profile of v0, /device:TPU:0, one launch (start us, length us, event | category | flops | bytes accessed | tf_op | source)
XLA Modules:
  0.0 501.3 jit_solution(12382191441929231244)
XLA Ops:
  7.2 2.6 pad_maximum_fusion.10
  11.0 113.4 %all-gather.2.cloned.1.call-done = bf16[2,2,256,5120]{3,2,1,0:T(8,128)(2,1)} async-done(((bf16[2,2,256,640]{3,2,1,0:T(8,128)(2,1)}), bf16[2,2,256,5120]{3,2,1,0:T(8,128)(2,1)}) %all-gather.2.cloned.1.call-update) | async-done | bytes 10485776 | tf_op jit(solution)/shard_map/all_gather | solution.py:63
  124.4 8.7 %fusion.81 = (bf16[1,2,256,5120]{3,2,1,0:T(8,128)(2,1)}, bf16[1,2,256,5120]{3,2,1,0:T(8,128)(2,1)}) fusion(bf16[2,2,256,5120]{3,2,1,0:T(8,128)(2,1)} %all-gather.2.cloned.1.call-done), kind=kLoop, calls=%fused_computation.105 | loop fusion | bytes 20971520 | tf_op jit(solution)/shard_map/slice | solution.py:67
  133.1 6.5 %fusion.49 = (bf16[2,4,64,320]{3,2,1,0:T(8,128)(2,1)}, f32[2,4,64,320]{3,2,1,0:T(8,128)}) fusion(f32[4,320]{1,0:T(4,128)S(1)} %fusion.65, bf16[2,4,64,5120]{3,2,1,0:T(8,128)(2,1)} %bitcast.132, bf16[5120,320]{0,1:T(8,128)(2,1)S(1)} %copy-done), kind=kOutput, calls=%fused_computation.58 | convolution fusion | flops 1679360000 | bytes 9507840 | tf_op jit(solution)/shard_map/dot_general | solution.py:119
  141.8 5.7 %fusion.44 = bf16[512,320]{0,1:T(8,128)(2,1)S(1)} fusion(bf16[512,5120]{1,0:T(8,128)(2,1)} %bitcast.130, bf16[320,5120]{1,0:T(8,128)(2,1)} %param.19, f32[512,320]{0,1:T(8,128)} %copy.145), kind=kOutput, calls=%fused_computation.48 | convolution fusion | flops 1680834560 | bytes 9502720 | tf_op jit(solution)/shard_map/dot_general | solution.py:36
  148.3 4.7 convolution_convert_fusion
  153.0 13.6 %copy.192 = bf16[1,2,256,5120]{2,1,0,3:T(2,128)(2,1)} copy(bf16[1,2,256,5120]{3,2,1,0:T(8,128)(2,1)} %bitcast.137) | data formatting | bytes 10485760
  166.6 5.7 %copy.200 = bf16[640,8,2,256]{3,1,2,0:T(8,128)(2,1)} copy(bf16[640,8,2,256]{3,2,1,0:T(2,128)(2,1)} %bitcast.135) | data formatting | bytes 10485760
  174.5 2.4 collective-permute-start.1
  176.9 4.2 collective-permute-start
  186.1 9.1 %collective-permute-done = bf16[2,256,640]{1,2,0:T(8,128)(2,1)} collective-permute-done((bf16[2,256,640]{1,2,0:T(8,128)(2,1)}, bf16[2,256,640]{1,2,0:T(8,128)(2,1)}, u32[]{:S(2)}, u32[]{:S(2)}) %collective-permute-start) | collective-permute-done | bytes 655392 | tf_op jit(solution)/shard_map/ppermute | solution.py:14
  200.6 2.6 fusion.84
  204.6 2.6 copy-done.27
  209.5 4.4 fusion.85
  213.9 4.9 add_convert_fusion
  218.8 13.6 %copy.190 = bf16[1,2,256,5120]{2,1,0,3:T(2,128)(2,1)} copy(bf16[1,2,256,5120]{3,2,1,0:T(8,128)(2,1)} %bitcast.129) | data formatting | bytes 10485760
  232.4 5.7 %copy.199 = bf16[640,8,2,256]{3,1,2,0:T(8,128)(2,1)} copy(bf16[640,8,2,256]{3,2,1,0:T(2,128)(2,1)} %bitcast.136) | data formatting | bytes 10485760
  238.2 11.3 %reshape.134 = bf16[512,16,320]{2,1,0:T(8,128)(2,1)} reshape(bf16[1,2,256,5120]{3,2,1,0:T(8,128)(2,1)} %get-tuple-element.54) | data formatting | bytes 10485760 | tf_op jit(solution)/shard_map/reshape;reshape;squeeze | solution.py:140
  249.5 11.0 %reshape.135 = bf16[512,16,320]{2,1,0:T(8,128)(2,1)} reshape(bf16[1,2,256,5120]{3,2,1,0:T(8,128)(2,1)} %get-tuple-element.55) | data formatting | bytes 10485760 | tf_op jit(solution)/shard_map/reshape;reshape;squeeze | solution.py:143
  260.7 8.6 %copy.186 = bf16[512,16,320]{0,2,1:T(8,128)(2,1)} copy(bf16[512,16,320]{2,1,0:T(8,128)(2,1)} %reshape.134) | data formatting | bytes 10485760 | tf_op jit(solution)/shard_map/reshape;reshape;squeeze | solution.py:140
  270.4 7.9 %convert_bitcast_fusion = bf16[16,320,320]{1,2,0:T(8,128)(2,1)} fusion(bf16[512,16,320]{0,2,1:T(8,128)(2,1)} %copy.186, bf16[512,320,1]{1,0,2:T(8,128)(2,1)} %bitcast.171), kind=kOutput, calls=%fused_computation.16 | convolution fusion | flops 1679360000 | bytes 8847360 | tf_op jit(solution)/shard_map/rk,rjn->jkn/dot_general | solution.py:147
  278.3 7.5 %fusion.23 = bf16[16,320,320]{1,2,0:T(8,128)(2,1)} fusion(bf16[512,16,320]{2,1,0:T(8,128)(2,1)} %reshape.135, bf16[512,320]{0,1:T(8,128)(2,1)S(1)} %copy-done.18), kind=kOutput, calls=%fused_computation.25 | convolution fusion | flops 1679360000 | bytes 8847360 | tf_op jit(solution)/shard_map/rjk,rn->jkn/dot_general | solution.py:141
  285.8 6.3 %fusion.9 = bf16[16,640,320]{1,2,0:T(8,128)(2,1)} fusion(bf16[512,16,320]{0,2,1:T(8,128)(2,1)S(1)} %bitcast.141, bf16[512,640]{0,1:T(8,128)(2,1)S(1)} %bitcast.152), kind=kOutput, calls=%fused_computation.15 | convolution fusion | flops 3358720000 | bytes 12451840 | tf_op jit(solution)/shard_map/rk,rjn->jkn/dot_general | solution.py:155
  292.1 22.7 %concatenate.27 = bf16[16,1288,320]{1,2,0:T(8,128)(2,1)} concatenate(bf16[16,640,320]{1,2,0:T(8,128)(2,1)} %fusion.9, bf16[16,320,320]{1,2,0:T(8,128)(2,1)} %fusion.23, bf16[16,320,320]{1,2,0:T(8,128)(2,1)} %convert_bitcast_fusion, bf16[16,8,320]{1,2,0:T(8,128)(2,1)S(1)} %copy.169), dimensions={1} | concatenate | bytes 26378240 | tf_op jit(solution)/shard_map/concatenate | solution.py:164
  314.9 9.6 %convolution_convert_fusion.2 = bf16[512,640]{1,0:T(8,128)(2,1)} fusion(bf16[512,5120]{1,0:T(8,128)(2,1)} %bitcast.131, bf16[640,5120]{1,0:T(8,128)(2,1)} %param.17), kind=kOutput, calls=%fused_computation.36 | convolution fusion | flops 3355770880 | bytes 12451840 | tf_op jit(solution)/shard_map/dot_general | solution.py:36
  327.6 5.0 fusion.26
  335.6 4.4 fusion.31
  340.1 14.9 %fusion.13 = f32[2,5,768,128]{2,3,1,0:T(8,128)} fusion(bf16[2,256,5,128]{1,3,2,0:T(8,128)(2,1)S(1)} %bitcast.148, f32[2,5,256,768]{2,3,1,0:T(8,128)} %fusion.31, f32[2,5,256,768]{2,3,1,0:T(8,128)} %copy-done.27, f32[2,5,256]{2,1,0:T(8,128)S(1)} %get-tuple-element.62), kind=kOutput, calls=%fused_computation.17 | convolution fusion | flops 517082368 | bytes 20326400 | tf_op jit(solution)/shard_map/shqk,sqhe->skhe/dot_general | solution.py:193
  355.0 2.5 slice_reduce_fusion.3
  365.1 14.1 %fusion.35 = bf16[2,5,128,256]{3,2,1,0:T(8,128)(2,1)} fusion(f32[2,5,256,768]{2,3,1,0:T(8,128)} %fusion.31, bf16[2,256,5,128]{3,1,2,0:T(8,128)(2,1)S(1)} %copy.140, bf16[2,256,5,128]{3,1,2,0:T(8,128)(2,1)S(1)} %copy-done.9, bf16[2,256,5,128]{3,1,2,0:T(8,128)(2,1)S(1)} %copy-done.11, f32[2,5,256,768]{2,3,1,0:T(8,128)} %copy-done.27, ...), kind=kOutput, calls=%fused_computation.35 | convolution fusion | flops 523308288 | bytes 18360320 | tf_op jit(solution)/shard_map/shqk,skhe->sqhe/dot_general | solution.py:189
  394.4 3.2 add_convert_fusion.1
  397.6 88.6 %reduce-scatter.8.cloned.1.call-done = bf16[1,1288,320]{1,2,0:T(8,128)(2,1)} async-done(((bf16[16,1288,320]{1,2,0:T(8,128)(2,1)}), bf16[1,1288,320]{1,2,0:T(8,128)(2,1)}) %reduce-scatter.8.cloned.1.call-update) | async-done | bytes 824336 | tf_op jit(solution)/shard_map/reduce_scatter | solution.py:163
  (131 shorter events, 57.6 us)
Async XLA Ops:
  7.2 125.9 %copy-start = (bf16[5120,320]{0,1:T(8,128)(2,1)S(1)}, bf16[5120,320]{0,1:T(8,128)(2,1)}, u32[]{:S(2)}) copy-start(bf16[5120,320]{0,1:T(8,128)(2,1)} %param.18) | copy-start | bytes 9830404
  7.2 117.2 %all-gather.2.cloned.1.call-start = ((), (), s32[]{:S(2)}) async-start(), calls=%async_computation.3 | async-start | bytes 11796480 | tf_op jit(solution)/shard_map/all_gather | solution.py:63
  9.9 376.5 %reduce-scatter.12.cloned.1.call-start = ((), (), s32[]{:S(2)}) async-start(), calls=%async_computation.6 | async-start | bytes 5898240
  172.3 8.8 %copy-start.24 = (bf16[1,2,256,640]{3,2,1,0:T(8,128)(2,1)S(1)}, bf16[1,2,256,640]{3,2,1,0:T(8,128)(2,1)}, u32[]{:S(2)}) copy-start(bf16[1,2,256,640]{3,2,1,0:T(8,128)(2,1)} %param.15) | copy-start | bytes 1966084
  172.3 9.1 %copy-start.25 = (bf16[1,2,256,640]{3,2,1,0:T(8,128)(2,1)S(1)}, bf16[1,2,256,640]{3,2,1,0:T(8,128)(2,1)}, u32[]{:S(2)}) copy-start(bf16[1,2,256,640]{3,2,1,0:T(8,128)(2,1)} %param.13) | copy-start | bytes 1966084
  172.3 218.1 %reduce-scatter.10.cloned.1.call-start = ((), (), s32[]{:S(2)}) async-start(), calls=%async_computation.5 | async-start | bytes 5898240
  174.5 9.6 %collective-permute-start.1 = (bf16[2,256,640]{1,2,0:T(8,128)(2,1)}, bf16[2,256,640]{1,2,0:T(8,128)(2,1)}, u32[]{:S(2)}, u32[]{:S(2)}) collective-permute-start(bf16[2,256,640]{1,2,0:T(8,128)(2,1)} %bitcast), channel_id=1, source_target_pairs={{0,8},{8,16},{16,24},{24,32},{32,40},{40,48},{48,56},{56,64},{64,7... | collective-permute-start | bytes 1966088 | tf_op jit(solution)/shard_map/ppermute | solution.py:14
  176.9 18.3 %collective-permute-start = (bf16[2,256,640]{1,2,0:T(8,128)(2,1)}, bf16[2,256,640]{1,2,0:T(8,128)(2,1)}, u32[]{:S(2)}, u32[]{:S(2)}) collective-permute-start(bf16[2,256,640]{1,2,0:T(8,128)(2,1)} %bitcast), channel_id=1, source_target_pairs={{0,16},{8,24},{16,32},{24,40},{32,48},{40,56},{48,64},{56,72},{64,... | collective-permute-start | bytes 1966088 | tf_op jit(solution)/shard_map/ppermute | solution.py:14
  203.3 4.2 copy-start.12
  203.4 4.4 copy-start.14
  203.4 5.3 %slice-start = ((s8[6553600]{0:T(1024)(128)(4,1)}), s8[4194304]{0:T(1024)(128)(4,1)S(1)}, s32[]{:S(2)}) async-start(s8[6553600]{0:T(1024)(128)(4,1)} %bitcast.138), calls=%async_computation.7 | async-start | bytes 8388608
  203.4 6.0 %slice-start.1 = ((s8[6553600]{0:T(1024)(128)(4,1)}), s8[2359296]{0:T(1024)(128)(4,1)S(1)}, s32[]{:S(2)}) async-start(s8[6553600]{0:T(1024)(128)(4,1)} %bitcast.138), calls=%async_computation.8 | async-start | bytes 4718592
  208.6 5.3 %copy-start.5 = (bf16[80,8,2,256]{3,1,2,0:T(8,128)(2,1)}, bf16[80,8,2,256]{3,1,2,0:T(8,128)(2,1)S(1)}, u32[]{:S(2)}) copy-start(bf16[80,8,2,256]{3,1,2,0:T(8,128)(2,1)S(1)} %copy.198) | copy-start | bytes 1966084
  209.5 4.4 copy-start.2
  209.5 4.4 copy-start.3
  238.2 248.0 %reduce-scatter.8.cloned.1.call-start = ((), (), s32[]{:S(2)}) async-start(), calls=%async_computation.4 | async-start | bytes 15319040 | tf_op jit(solution)/shard_map/reduce_scatter | solution.py:163
  249.5 11.0 %copy-start.17 = (bf16[512,320]{0,1:T(8,128)(2,1)S(1)}, bf16[512,320]{0,1:T(8,128)(2,1)}, u32[]{:S(2)}) copy-start(bf16[512,320]{0,1:T(8,128)(2,1)} %copy-done.16) | copy-start | bytes 983044
  260.7 8.7 %copy-start.26 = (s32[1,4]{1,0:T(1,128)S(1)}, s32[1,4]{1,0:T(1,128)}, u32[]{:S(2)}) copy-start(s32[1,4]{1,0:T(1,128)} %param.21) | copy-start | bytes 52
  270.3 7.9 %copy-start.18 = (bf16[512,320]{0,1:T(8,128)(2,1)S(1)}, bf16[512,320]{0,1:T(8,128)(2,1)}, u32[]{:S(2)}) copy-start(bf16[512,320]{0,1:T(8,128)(2,1)} %copy-done.16) | copy-start | bytes 983044
  270.4 15.5 %slice-start.2 = ((s8[5242880]{0:T(1024)(128)(4,1)}), s8[4194304]{0:T(1024)(128)(4,1)S(1)}, s32[]{:S(2)}) async-start(s8[5242880]{0:T(1024)(128)(4,1)} %bitcast.140), calls=%async_computation.9 | async-start | bytes 8388608
  278.3 7.5 %slice-start.3 = ((s8[5242880]{0:T(1024)(128)(4,1)}), s8[1048576]{0:T(1024)(128)(4,1)S(1)}, s32[]{:S(2)}) async-start(s8[5242880]{0:T(1024)(128)(4,1)} %bitcast.140), calls=%async_computation.10 | async-start | bytes 2097152
  278.3 7.5 %copy-start.6 = (bf16[80,8,2,256]{3,1,2,0:T(8,128)(2,1)S(1)}, bf16[80,8,2,256]{3,1,2,0:T(8,128)(2,1)}, u32[]{:S(2)}) copy-start(bf16[80,8,2,256]{3,1,2,0:T(8,128)(2,1)} %copy-done.5) | copy-start | bytes 1966084
  327.6 8.0 %copy-start.7 = (bf16[2,256,5,128]{1,3,2,0:T(8,128)(2,1)S(1)}, bf16[2,256,5,128]{1,3,2,0:T(8,128)(2,1)}, u32[]{:S(2)}) copy-start(bf16[2,256,5,128]{1,3,2,0:T(8,128)(2,1)} %copy.161) | copy-start | bytes 1966084
  327.6 8.0 %copy-start.13 = (bf16[2,256,5,128]{1,3,2,0:T(8,128)(2,1)S(1)}, bf16[2,256,5,128]{1,3,2,0:T(8,128)(2,1)}, u32[]{:S(2)}) copy-start(bf16[2,256,5,128]{1,3,2,0:T(8,128)(2,1)} %copy-done.12) | copy-start | bytes 1966084
  327.6 8.0 %copy-start.15 = (bf16[2,256,5,128]{1,3,2,0:T(8,128)(2,1)S(1)}, bf16[2,256,5,128]{1,3,2,0:T(8,128)(2,1)}, u32[]{:S(2)}) copy-start(bf16[2,256,5,128]{1,3,2,0:T(8,128)(2,1)} %copy-done.14) | copy-start | bytes 1966084
  340.1 17.4 %copy-start.20 = (bf16[256,640]{0,1:T(8,128)(2,1)S(1)}, bf16[256,640]{0,1:T(8,128)(2,1)}, u32[]{:S(2)}) copy-start(bf16[256,640]{0,1:T(8,128)(2,1)} %get-tuple-element.53) | copy-start | bytes 983044
  340.1 19.6 %copy-start.19 = (bf16[256,640]{0,1:T(8,128)(2,1)S(1)}, bf16[256,640]{0,1:T(8,128)(2,1)}, u32[]{:S(2)}) copy-start(bf16[256,640]{0,1:T(8,128)(2,1)} %get-tuple-element.52) | copy-start | bytes 983044
  355.0 10.1 %copy-start.9 = (bf16[2,256,5,128]{3,1,2,0:T(8,128)(2,1)S(1)}, bf16[2,256,5,128]{3,1,2,0:T(8,128)(2,1)}, u32[]{:S(2)}) copy-start(bf16[2,256,5,128]{3,1,2,0:T(8,128)(2,1)} %copy-done.8) | copy-start | bytes 1966084
  355.0 10.1 %copy-start.11 = (bf16[2,256,5,128]{3,1,2,0:T(8,128)(2,1)S(1)}, bf16[2,256,5,128]{3,1,2,0:T(8,128)(2,1)}, u32[]{:S(2)}) copy-start(bf16[2,256,5,128]{3,1,2,0:T(8,128)(2,1)} %copy-done.10) | copy-start | bytes 1966084
  358.4 25.1 %collective-permute-start.3 = (bf16[2,256,640]{1,2,0:T(8,128)(2,1)}, bf16[2,256,640]{1,2,0:T(8,128)(2,1)}, u32[]{:S(2)}, u32[]{:S(2)}) collective-permute-start(bf16[2,256,640]{1,2,0:T(8,128)(2,1)} %pad_maximum_fusion.14), channel_id=1, source_target_pairs={{16,0},{24,8},{32,16},{40,24},{48,32},{56,40},{64,48},{72,56},{80,... | collective-permute-start | bytes 1966088 | tf_op jit(solution)/shard_map/ppermute | solution.py:14
  360.6 22.9 %collective-permute-start.2 = (bf16[2,256,640]{1,2,0:T(8,128)(2,1)}, bf16[2,256,640]{1,2,0:T(8,128)(2,1)}, u32[]{:S(2)}, u32[]{:S(2)}) collective-permute-start(bf16[2,256,640]{1,2,0:T(8,128)(2,1)} %pad_maximum_fusion.13), channel_id=1, source_target_pairs={{8,0},{16,8},{24,16},{32,24},{40,32},{48,40},{56,48},{64,56},{72,6... | collective-permute-start | bytes 1966088 | tf_op jit(solution)/shard_map/ppermute | solution.py:14
  394.4 99.9 %copy-start.1 = (bf16[5120,320]{0,1:T(8,128)(2,1)S(1)}, bf16[5120,320]{0,1:T(8,128)(2,1)}, u32[]{:S(2)}) copy-start(bf16[5120,320]{0,1:T(8,128)(2,1)} %param.18) | copy-start | bytes 9830404
  (8 other events, 16.8 us)
Sparse Core Ops, SparseCore 0:
  10.2 114.0 all-gather.1
  172.4 81.6 reduce-scatter.11
  256.5 70.4 reduce-scatter.9
  331.4 154.7 reduce-scatter.7
where the time goes:
time: 511 us; the launch traced here: 501 us
  waiting for transfers between devices  211 us (41%)
  local copies, waits for them, and re-layouts  149 us (29%)
  matrix products  99.7 us (20%)
  other arithmetic  16.6 us (3%)
  between operations  15.5 us (3%)
  starting transfers between devices  9.37 us (2%)
    all_gather x1, waiting for transfers between devices, body(): lax.all_gather(jnp.concatenate([hidden_in, out_grad], axis=0), 'tensor',...  113 us
    reduce_scatter x1, waiting for transfers between devices, body(): lax.psum_scatter(jnp.concatenate(pieces, axis=1), 'tm', scatter_dimension...  88.6 us
    unnamed x84, local copies, waits for them, and re-layouts  68 us
    concatenate x1, local copies, waits for them, and re-layouts, body(): jnp.concatenate(pieces, axis=1)  22.7 us
    dot_general x3, matrix products, contract_cols(): lax.dot_general(left, right, (((1,), (1,)), ((), ())), preferred_element_...  20.1 us
    another operation x2, local copies, waits for them, and re-layouts, body(): grad_split = grad_rows.reshape(row_count, tm_count, col_block)  19.9 us
    dot_general x1, matrix products, body(): jnp.einsum('shqk,sqhe->skhe', score_grad, query_heads, preferred_element_...  14.9 us
    dot_general x1, matrix products, body(): jnp.einsum('shqk,skhe->sqhe', score_grad, key_heads, preferred_element_ty...  14.1 us
  transfers between devices with their start and end apart: 8, of which 3 were waited for; matrix products, arithmetic and copies ran while one was open for 40% of the time, Pallas kernels for 0%

commit v1 on v0

--- a/solution.py
+++ b/solution.py
@@ -6,6 +6,15 @@
 HD = 128
 GELU_C = 0.7978845608028654
 GELU_A = 0.044715
+
+
+def enter_marks(xx, array_dim):
+    buffers = []
+    for _ in range(jax.lax.axis_size("tensor")):
+        buffers.append(xx)
+    y1 = jnp.stack(buffers)
+    h_now = jax.lax.all_to_all(y1, axis_name="tensor", split_axis=0, concat_axis=0)
+    return jnp.concatenate(h_now, axis=array_dim)
 
 
 def from_behind(value, axis, steps):
@@ -60,9 +69,7 @@
     row_count = steps_here * tokens_here
     action_count = actions.shape[1]
     score_scale = HD ** (-0.5)
-    full_both = lax.all_gather(
-        jnp.concatenate([hidden_in, out_grad], axis=0), "tensor", axis=3, tiled=True
-    )
+    full_both = enter_marks(jnp.concatenate([hidden_in, out_grad], axis=0), 3)
     input_rows = full_both[0].reshape(row_count, model_width)
     grad_rows = full_both[1].reshape(row_count, model_width)
     own_cache = clean_cache[0]

time: 511 us -> 604 us (1.18)
  waiting for transfers between devices: 211 us -> 259 us
  local copies, waits for them, and re-layouts: 149 us -> 192 us
    all_to_all x0 -> x1, waiting for transfers between devices: none -> 117 us  [enter_marks(): jax.lax.all_to_all(y1, axis_name='tensor', split_axis=0, concat_axis=0)]
    all_gather x1 -> x0, waiting for transfers between devices: 113 us -> none  [body(): lax.all_gather(jnp.concatenate([hidden_in, out_grad], axis=0), 'tensor',...]
    reduce_scatter x1, waiting for transfers between devices: 88.6 us -> 133 us  [body(): lax.psum_scatter(jnp.concatenate(pieces, axis=1), 'tm', scatter_dimension...]
    slice x1 -> x3, local copies, waits for them, and re-layouts: 8.73 us -> 29.4 us  [body(): grad_rows = full_both[1].reshape(row_count, model_width)]
    slice x0 -> x2, local copies, waits for them, and re-layouts: none -> 19.1 us  [body(): input_rows = full_both[0].reshape(row_count, model_width)]
    another operation x2 -> x1, local copies, waits for them, and re-layouts: 19.9 us -> 9.31 us  [body(): grad_split = grad_rows.reshape(row_count, tm_count, col_block)]
    dot_general x0 -> x1, local copies, waits for them, and re-layouts: none -> 8.85 us  [body(): jnp.dot(input_rows, branch_in, preferred_element_type=jnp.float32)]
    unnamed x84 -> x91, local copies, waits for them, and re-layouts: 68 us -> 70.4 us
  transfers between devices with their start and end apart: 8 -> 8, of which waited for: 3 -> 3; matrix products, arithmetic and copies ran while one was open for 40% -> 35% of each run, Pallas kernels for 0% -> 0%
where the time goes in v1:
time: 604 us; the launch traced here: 593 us
  waiting for transfers between devices  259 us (43%)
  local copies, waits for them, and re-layouts  192 us (32%)
  matrix products  96.5 us (16%)
  other arithmetic  15.3 us (3%)
  between operations  15.2 us (3%)
  starting transfers between devices  15 us (2%)
    reduce_scatter x1, waiting for transfers between devices, body(): lax.psum_scatter(jnp.concatenate(pieces, axis=1), 'tm', scatter_dimension...  133 us
    all_to_all x1, waiting for transfers between devices, enter_marks(): jax.lax.all_to_all(y1, axis_name='tensor', split_axis=0, concat_axis=0)  117 us
    unnamed x91, local copies, waits for them, and re-layouts  70.4 us
    slice x3, local copies, waits for them, and re-layouts, body(): grad_rows = full_both[1].reshape(row_count, model_width)  29.4 us
    concatenate x1, local copies, waits for them, and re-layouts, body(): jnp.concatenate(pieces, axis=1)  22.6 us
    dot_general x3, matrix products, contract_cols(): lax.dot_general(left, right, (((1,), (1,)), ((), ())), preferred_element_...  20 us
    slice x2, local copies, waits for them, and re-layouts, body(): input_rows = full_both[0].reshape(row_count, model_width)  19.1 us
    dot_general x1, matrix products, body(): jnp.einsum('shqk,sqhe->skhe', score_grad, query_heads, preferred_element_...  14.4 us
  transfers between devices with their start and end apart: 8, of which 3 were waited for; matrix products, arithmetic and copies ran while one was open for 35% of the time, Pallas kernels for 0%

profile of v1, /device:TPU:0, one launch (start us, length us, event | category | flops | bytes accessed | tf_op | source)
XLA Modules:
  0.0 593.3 jit_solution(7581171617489251390)
XLA Ops:
  8.8 5.3 stack.35
  14.1 5.9 all-to-all-start
  20.2 116.7 %all-to-all-done = bf16[8,2,2,256,640]{4,3,2,1,0:T(8,128)(2,1)} async-done(((bf16[8,2,2,256,640]{4,3,2,1,0:T(8,128)(2,1)}), bf16[8,2,2,256,640]{4,3,2,1,0:T(8,128)(2,1)}, u32[]{:S(2)}, u32[]{:S(2)}) %all-to-all-start) | async-done | bytes 10485792 | tf_op jit(solution)/shard_map/all_to_all | solution.py:16
  136.9 9.6 %fusion.76 = (bf16[1,2,256,8,640]{4,2,1,0,3:T(8,128)(2,1)}, bf16[1,2,256,8,640]{4,2,1,0,3:T(8,128)(2,1)}) fusion(bf16[2,2,256,8,640]{4,2,1,0,3:T(8,128)(2,1)} %bitcast.12), kind=kLoop, calls=%fused_computation.103 | loop fusion | bytes 20971520 | tf_op jit(solution)/shard_map/slice | solution.py:74
  146.5 5.7 copy.194
  155.8 5.4 copy.188
  161.1 8.9 %dot_general.56 = bf16[2,4,64,5120]{3,2,1,0:T(8,128)(2,1)} reshape(bf16[1,2,256,8,640]{4,3,2,1,0:T(8,128)(2,1)} %copy.188) | data formatting | bytes 10485760 | tf_op jit(solution)/shard_map/dot_general | solution.py:126
  170.0 6.5 %fusion.44 = (bf16[2,4,64,320]{3,2,1,0:T(8,128)(2,1)}, f32[2,4,64,320]{3,2,1,0:T(8,128)}) fusion(f32[4,320]{1,0:T(4,128)S(1)} %fusion.60, bf16[2,4,64,5120]{3,2,1,0:T(8,128)(2,1)} %dot_general.56, bf16[5120,320]{0,1:T(8,128)(2,1)S(1)} %copy-done), kind=kOutput, calls=%fused_computation.56 | convolution fusion | flops 1679360000 | bytes 9507840 | tf_op jit(solution)/shard_map/dot_general | solution.py:126
  178.7 5.7 fusion.39
  185.2 4.7 convolution_convert_fusion
  189.8 13.6 %copy.235 = bf16[1,2,256,5120]{2,1,0,3:T(2,128)(2,1)} copy(bf16[1,2,256,5120]{3,2,1,0:T(8,128)(2,1)} %bitcast.142) | data formatting | bytes 10485760
  203.4 5.7 copy.244
  213.7 4.0 collective-permute-start
  222.7 9.4 %collective-permute-done = bf16[2,256,640]{1,2,0:T(8,128)(2,1)} collective-permute-done((bf16[2,256,640]{1,2,0:T(8,128)(2,1)}, bf16[2,256,640]{1,2,0:T(8,128)(2,1)}, u32[]{:S(2)}, u32[]{:S(2)}) %collective-permute-start) | collective-permute-done | bytes 655392 | tf_op jit(solution)/shard_map/ppermute | solution.py:23
  246.3 4.4 fusion.80
  250.8 4.8 add_convert_fusion
  255.6 13.7 %copy.233 = bf16[1,2,256,5120]{2,1,0,3:T(2,128)(2,1)} copy(bf16[1,2,256,5120]{3,2,1,0:T(8,128)(2,1)} %bitcast.136) | data formatting | bytes 10485760
  269.3 5.7 copy.243
  275.0 14.1 %copy.209 = bf16[1,2,256,8,640]{2,1,4,3,0:T(2,128)(2,1)} copy(bf16[1,2,256,8,640]{4,2,1,0,3:T(8,128)(2,1)} %get-tuple-element.64) | data formatting | bytes 10485760 | tf_op jit(solution)/shard_map/slice | solution.py:74
  289.2 13.7 %copy.211 = bf16[1,2,256,8,640]{2,1,4,3,0:T(2,128)(2,1)} copy(bf16[1,2,256,8,640]{4,2,1,0,3:T(8,128)(2,1)} %get-tuple-element.65) | data formatting | bytes 10485760 | tf_op jit(solution)/shard_map/slice | solution.py:73
  303.1 9.3 %reshape_reshape_squeeze.6 = bf16[512,16,320]{0,2,1:T(8,128)(2,1)} reshape(bf16[1,2,256,8,640]{2,1,4,3,0:T(2,128)(2,1)} %copy.209) | data formatting | bytes 10485760 | tf_op jit(solution)/shard_map/reshape;reshape;squeeze | solution.py:147
  312.4 9.2 %reshape_reshape_squeeze.7 = bf16[512,16,320]{0,2,1:T(8,128)(2,1)} reshape(bf16[1,2,256,8,640]{2,1,4,3,0:T(2,128)(2,1)} %copy.211) | data formatting | bytes 10485760 | tf_op jit(solution)/shard_map/reshape;reshape;squeeze | solution.py:150
  322.7 6.8 %convolution_convert_fusion.2 = bf16[16,320,320]{1,2,0:T(8,128)(2,1)} fusion(bf16[512,16,320]{0,2,1:T(8,128)(2,1)} %reshape_reshape_squeeze.7, bf16[512,320]{0,1:T(8,128)(2,1)} %copy-done.16), kind=kOutput, calls=%fused_computation.23 | convolution fusion | flops 1679360000 | bytes 8847360 | tf_op jit(solution)/shard_map/rjk,rn->jkn/dot_general | solution.py:148
  329.5 7.6 %convert_bitcast_fusion = bf16[16,320,320]{1,2,0:T(8,128)(2,1)} fusion(bf16[512,16,320]{0,2,1:T(8,128)(2,1)} %reshape_reshape_squeeze.6, bf16[512,320,1]{1,0,2:T(8,128)(2,1)S(1)} %bitcast.178), kind=kOutput, calls=%fused_computation.14 | convolution fusion | flops 1679360000 | bytes 8847360 | tf_op jit(solution)/shard_map/rk,rjn->jkn/dot_general | solution.py:154
  337.0 6.3 %fusion.7 = bf16[16,640,320]{1,2,0:T(8,128)(2,1)} fusion(bf16[512,16,320]{0,2,1:T(8,128)(2,1)S(1)} %bitcast.148, bf16[512,640]{0,1:T(8,128)(2,1)S(1)} %bitcast.159), kind=kOutput, calls=%fused_computation.13 | convolution fusion | flops 3358720000 | bytes 12451840 | tf_op jit(solution)/shard_map/rk,rjn->jkn/dot_general | solution.py:162
  343.3 22.6 %concatenate.27 = bf16[16,1288,320]{1,2,0:T(8,128)(2,1)} concatenate(bf16[16,640,320]{1,2,0:T(8,128)(2,1)} %fusion.7, bf16[16,320,320]{1,2,0:T(8,128)(2,1)} %convolution_convert_fusion.2, bf16[16,320,320]{1,2,0:T(8,128)(2,1)} %convert_bitcast_fusion, bf16[16,8,320]{1,2,0:T(8,128)(2,1)S(1)} %copy.214), dimensions={1} | concatenate | bytes 26378240 | tf_op jit(solution)/shard_map/concatenate | solution.py:171
  365.9 9.6 %convolution_convert_fusion.3 = bf16[512,640]{1,0:T(8,128)(2,1)} fusion(bf16[512,5120]{1,0:T(8,128)(2,1)} %bitcast.146, bf16[640,5120]{1,0:T(8,128)(2,1)} %param.17), kind=kOutput, calls=%fused_computation.34 | convolution fusion | flops 3355770880 | bytes 12451840 | tf_op jit(solution)/shard_map/dot_general | solution.py:45
  378.8 5.1 fusion.21
  387.0 4.4 fusion.26
  391.4 14.4 %fusion.11 = f32[2,5,768,128]{2,3,1,0:T(8,128)} fusion(bf16[2,256,5,128]{1,3,2,0:T(8,128)(2,1)S(1)} %bitcast.155, f32[2,5,256,768]{2,3,1,0:T(8,128)} %fusion.26, f32[2,5,256,768]{2,3,1,0:T(8,128)} %copy-done.28, f32[2,5,256]{2,1,0:T(8,128)S(1)} %get-tuple-element.72), kind=kOutput, calls=%fused_computation.15 | convolution fusion | flops 517082368 | bytes 20326400 | tf_op jit(solution)/shard_map/shqk,sqhe->skhe/dot_general | solution.py:200
  416.2 13.2 %fusion.30 = bf16[2,5,128,256]{3,2,1,0:T(8,128)(2,1)S(1)} fusion(f32[2,5,256,768]{2,3,1,0:T(8,128)} %fusion.26, bf16[2,256,5,128]{3,1,2,0:T(8,128)(2,1)S(1)} %copy.183, bf16[2,256,5,128]{3,1,2,0:T(8,128)(2,1)S(1)} %copy-done.9, bf16[2,256,5,128]{3,1,2,0:T(8,128)(2,1)S(1)} %copy-done.11, f32[2,5,256,768]{2,3,1,0:T(8,128)} %copy-done.28, ...), kind=kOutput, calls=%fused_computation.33 | convolution fusion | flops 523308288 | bytes 18360320 | tf_op jit(solution)/shard_map/shqk,skhe->sqhe/dot_general | solution.py:196
  445.8 132.6 %reduce-scatter.8.cloned.1.call-done = bf16[1,1288,320]{1,2,0:T(8,128)(2,1)} async-done(((bf16[16,1288,320]{1,2,0:T(8,128)(2,1)}), bf16[1,1288,320]{1,2,0:T(8,128)(2,1)}) %reduce-scatter.8.cloned.1.call-update) | async-done | bytes 824336 | tf_op jit(solution)/shard_map/reduce_scatter | solution.py:170
  (143 shorter events, 73.6 us)
Async XLA Ops:
  7.2 162.8 %copy-start = (bf16[5120,320]{0,1:T(8,128)(2,1)S(1)}, bf16[5120,320]{0,1:T(8,128)(2,1)}, u32[]{:S(2)}) copy-start(bf16[5120,320]{0,1:T(8,128)(2,1)} %param.18) | copy-start | bytes 9830404
  14.1 5.9 %copy-start.25 = (s32[1,4]{1,0:T(1,128)S(1)}, s32[1,4]{1,0:T(1,128)}, u32[]{:S(2)}) copy-start(s32[1,4]{1,0:T(1,128)} %param.21) | copy-start | bytes 52
  14.1 6.0 %copy-start.26 = (bf16[128,320]{0,1:T(8,128)(2,1)S(1)}, bf16[128,320]{0,1:T(8,128)(2,1)}, u32[]{:S(2)}) copy-start(bf16[128,320]{0,1:T(8,128)(2,1)} %param.20) | copy-start | bytes 245764
  14.1 122.8 %all-to-all-start = ((bf16[8,2,2,256,640]{4,3,2,1,0:T(8,128)(2,1)}), bf16[8,2,2,256,640]{4,3,2,1,0:T(8,128)(2,1)}, u32[]{:S(2)}, u32[]{:S(2)}) async-start(bf16[8,2,2,256,640]{4,3,2,1,0:T(8,128)(2,1)} %stack.35), calls=%async_computation | async-start | bytes 20971520 | tf_op jit(solution)/shard_map/all_to_all | solution.py:16
  20.0 414.5 %reduce-scatter.12.cloned.1.call-start = ((), (), s32[]{:S(2)}) async-start(), calls=%async_computation.6 | async-start | bytes 5898240
  146.5 9.2 %slice-start = ((s8[5242880]{0:T(1024)(128)(4,1)}), s8[4194304]{0:T(1024)(128)(4,1)S(1)}, s32[]{:S(2)}) async-start(s8[5242880]{0:T(1024)(128)(4,1)} %bitcast.134), calls=%async_computation.7 | async-start | bytes 8388608
  209.1 9.3 %copy-start.23 = (bf16[1,2,256,640]{3,2,1,0:T(8,128)(2,1)S(1)}, bf16[1,2,256,640]{3,2,1,0:T(8,128)(2,1)}, u32[]{:S(2)}) copy-start(bf16[1,2,256,640]{3,2,1,0:T(8,128)(2,1)} %param.13) | copy-start | bytes 1966084
  209.1 9.5 %copy-start.24 = (bf16[1,2,256,640]{3,2,1,0:T(8,128)(2,1)S(1)}, bf16[1,2,256,640]{3,2,1,0:T(8,128)(2,1)}, u32[]{:S(2)}) copy-start(bf16[1,2,256,640]{3,2,1,0:T(8,128)(2,1)} %param.14) | copy-start | bytes 1966084
  209.1 229.4 %reduce-scatter.10.cloned.1.call-start = ((), (), s32[]{:S(2)}) async-start(), calls=%async_computation.5 | async-start | bytes 5898240
  211.3 9.3 %collective-permute-start.1 = (bf16[2,256,640]{1,2,0:T(8,128)(2,1)}, bf16[2,256,640]{1,2,0:T(8,128)(2,1)}, u32[]{:S(2)}, u32[]{:S(2)}) collective-permute-start(bf16[2,256,640]{1,2,0:T(8,128)(2,1)} %bitcast), channel_id=1, source_target_pairs={{0,8},{8,16},{16,24},{24,32},{32,40},{40,48},{48,56},{56,64},{64,7... | collective-permute-start | bytes 1966088 | tf_op jit(solution)/shard_map/ppermute | solution.py:23
  213.7 18.4 %collective-permute-start = (bf16[2,256,640]{1,2,0:T(8,128)(2,1)}, bf16[2,256,640]{1,2,0:T(8,128)(2,1)}, u32[]{:S(2)}, u32[]{:S(2)}) collective-permute-start(bf16[2,256,640]{1,2,0:T(8,128)(2,1)} %bitcast), channel_id=1, source_target_pairs={{0,16},{8,24},{16,32},{24,40},{32,48},{40,56},{48,64},{56,72},{64,... | collective-permute-start | bytes 1966088 | tf_op jit(solution)/shard_map/ppermute | solution.py:23
  240.3 5.3 slice-start.2
  240.3 6.0 %slice-start.3 = ((s8[6553600]{0:T(1024)(128)(4,1)}), s8[2359296]{0:T(1024)(128)(4,1)S(1)}, s32[]{:S(2)}) async-start(s8[6553600]{0:T(1024)(128)(4,1)} %bitcast.143), calls=%async_computation.10 | async-start | bytes 4718592
  245.5 5.3 copy-start.5
  246.3 4.4 copy-start.2
  246.3 4.4 copy-start.3
  275.0 303.5 %reduce-scatter.8.cloned.1.call-start = ((), (), s32[]{:S(2)}) async-start(), calls=%async_computation.4 | async-start | bytes 15319040 | tf_op jit(solution)/shard_map/reduce_scatter | solution.py:170
  289.2 13.7 %copy-start.17 = (bf16[512,320]{0,1:T(8,128)(2,1)S(1)}, bf16[512,320]{0,1:T(8,128)(2,1)}, u32[]{:S(2)}) copy-start(bf16[512,320]{0,1:T(8,128)(2,1)} %copy-done.16) | copy-start | bytes 983044
  322.6 6.8 %copy-start.27 = (bf16[2,4,64,320]{3,2,1,0:T(8,128)(2,1)S(1)}, bf16[2,4,64,320]{3,2,1,0:T(8,128)(2,1)}, u32[]{:S(2)}) copy-start(bf16[2,4,64,320]{3,2,1,0:T(8,128)(2,1)} %get-tuple-element.74) | copy-start | bytes 983044
  322.6 14.4 %slice-start.4 = ((s8[5242880]{0:T(1024)(128)(4,1)}), s8[4194304]{0:T(1024)(128)(4,1)S(1)}, s32[]{:S(2)}) async-start(s8[5242880]{0:T(1024)(128)(4,1)} %bitcast.147), calls=%async_computation.11 | async-start | bytes 8388608
  329.5 7.6 %slice-start.5 = ((s8[5242880]{0:T(1024)(128)(4,1)}), s8[1048576]{0:T(1024)(128)(4,1)S(1)}, s32[]{:S(2)}) async-start(s8[5242880]{0:T(1024)(128)(4,1)} %bitcast.147), calls=%async_computation.12 | async-start | bytes 2097152
  329.5 7.6 %copy-start.6 = (bf16[80,8,2,256]{3,1,2,0:T(8,128)(2,1)S(1)}, bf16[80,8,2,256]{3,1,2,0:T(8,128)(2,1)}, u32[]{:S(2)}) copy-start(bf16[80,8,2,256]{3,1,2,0:T(8,128)(2,1)} %copy-done.5) | copy-start | bytes 1966084
  378.8 8.2 %copy-start.7 = (bf16[2,256,5,128]{1,3,2,0:T(8,128)(2,1)S(1)}, bf16[2,256,5,128]{1,3,2,0:T(8,128)(2,1)}, u32[]{:S(2)}) copy-start(bf16[2,256,5,128]{1,3,2,0:T(8,128)(2,1)} %copy.206) | copy-start | bytes 1966084
  378.8 8.2 %copy-start.13 = (bf16[2,256,5,128]{1,3,2,0:T(8,128)(2,1)S(1)}, bf16[2,256,5,128]{1,3,2,0:T(8,128)(2,1)}, u32[]{:S(2)}) copy-start(bf16[2,256,5,128]{1,3,2,0:T(8,128)(2,1)} %copy-done.12) | copy-start | bytes 1966084
  378.8 8.2 %copy-start.15 = (bf16[2,256,5,128]{1,3,2,0:T(8,128)(2,1)S(1)}, bf16[2,256,5,128]{1,3,2,0:T(8,128)(2,1)}, u32[]{:S(2)}) copy-start(bf16[2,256,5,128]{1,3,2,0:T(8,128)(2,1)} %copy-done.14) | copy-start | bytes 1966084
  391.4 16.5 %copy-start.19 = (bf16[256,640]{0,1:T(8,128)(2,1)S(1)}, bf16[256,640]{0,1:T(8,128)(2,1)}, u32[]{:S(2)}) copy-start(bf16[256,640]{0,1:T(8,128)(2,1)} %get-tuple-element.63) | copy-start | bytes 983044
  391.4 18.7 %copy-start.18 = (bf16[256,640]{0,1:T(8,128)(2,1)S(1)}, bf16[256,640]{0,1:T(8,128)(2,1)}, u32[]{:S(2)}) copy-start(bf16[256,640]{0,1:T(8,128)(2,1)} %get-tuple-element.62) | copy-start | bytes 983044
  405.9 10.3 %copy-start.9 = (bf16[2,256,5,128]{3,1,2,0:T(8,128)(2,1)S(1)}, bf16[2,256,5,128]{3,1,2,0:T(8,128)(2,1)}, u32[]{:S(2)}) copy-start(bf16[2,256,5,128]{3,1,2,0:T(8,128)(2,1)} %copy-done.8) | copy-start | bytes 1966084
  405.9 10.3 %copy-start.11 = (bf16[2,256,5,128]{3,1,2,0:T(8,128)(2,1)S(1)}, bf16[2,256,5,128]{3,1,2,0:T(8,128)(2,1)}, u32[]{:S(2)}) copy-start(bf16[2,256,5,128]{3,1,2,0:T(8,128)(2,1)} %copy-done.10) | copy-start | bytes 1966084
  408.9 22.7 %collective-permute-start.3 = (bf16[2,256,640]{1,2,0:T(8,128)(2,1)}, bf16[2,256,640]{1,2,0:T(8,128)(2,1)}, u32[]{:S(2)}, u32[]{:S(2)}) collective-permute-start(bf16[2,256,640]{1,2,0:T(8,128)(2,1)} %pad_maximum_fusion.14), channel_id=1, source_target_pairs={{16,0},{24,8},{32,16},{40,24},{48,32},{56,40},{64,48},{72,56},{80,... | collective-permute-start | bytes 1966088 | tf_op jit(solution)/shard_map/ppermute | solution.py:23
  411.1 20.6 %collective-permute-start.2 = (bf16[2,256,640]{1,2,0:T(8,128)(2,1)}, bf16[2,256,640]{1,2,0:T(8,128)(2,1)}, u32[]{:S(2)}, u32[]{:S(2)}) collective-permute-start(bf16[2,256,640]{1,2,0:T(8,128)(2,1)} %pad_maximum_fusion.13), channel_id=1, source_target_pairs={{8,0},{16,8},{24,16},{32,24},{40,32},{48,40},{56,48},{64,56},{72,6... | collective-permute-start | bytes 1966088 | tf_op jit(solution)/shard_map/ppermute | solution.py:23
  442.5 144.1 %copy-start.1 = (bf16[5120,320]{0,1:T(8,128)(2,1)S(1)}, bf16[5120,320]{0,1:T(8,128)(2,1)}, u32[]{:S(2)}) copy-start(bf16[5120,320]{0,1:T(8,128)(2,1)} %param.18) | copy-start | bytes 9830404
  (11 other events, 29.0 us)
Sparse Core Ops, SparseCore 0:
  209.2 121.2 reduce-scatter.11
  333.0 72.7 reduce-scatter.9
  410.3 168.1 reduce-scatter.7
